TPU v7x, 128 devices: a whole 4x4x4 slice. The times are simulated.
128 devices in a mesh: dp: 32 (over y, z, x_hi), mp: 4 (over x_lo, core).
Axes of the slice: x: 4 (x_hi: 2, x_lo: 2; x = x_hi * 2 + x_lo), y: 4, z: 4, core: 2. Of those that a mesh axis runs over, the one named last changes fastest.
Arguments:
- tokens: bfloat16 [8192, 2048], P('dp'), may hold values from -6 to 6
- lengths: int32 [4], replicated, may hold values from 1 to 4096, 8192 in all
- w_query: float32 [2048, 2048], P('dp', 'mp')
- w_key: float32 [2048, 2048], P('dp', 'mp')
- w_value: float32 [2048, 2048], P('dp', 'mp'), may hold values from -0.125 to 0.125
- w_out: float32 [2048, 2048], P('dp', 'mp'), may hold values from -0.125 to 0.125
- w_gate: float32 [2048, 4096], P('dp', 'mp'), may hold values from -0.125 to 0.125
- w_up: float32 [2048, 4096], P('dp', 'mp'), may hold values from -0.125 to 0.125
- w_down: float32 [4096, 2048], P('dp', 'mp'), may hold values from -0.09375 to 0.09375
Outputs:
- layer_out: bfloat16 [8192, 2048], P(('dp', 'mp'))
Inputs may be any that keep to these rules, and one draw needn't show every extreme that they name: Every prompt is 1 to 4096 tokens long and one is exactly 4096; the lengths sum to 8192.
All inputs are finite; a program needn't handle non-finite values.
Results may differ from a plain program's by a relative error of at most 0.02.
The roundings to bfloat16 on the way count: a program that leaves them out, or rounds other values in their place, can miss the bound.
Values may be sent and summed in bfloat16 or wider, within the bound.
No kernel may reach another device: no remote copies, remote signals or barrier semaphores. Data moves between devices by JAX's collectives and lax.ppermute only.
A program may use at most 128 MiB of HBM per device.

v0:
```python
import jax
import jax.numpy as jnp
from jax import lax
from jax.sharding import Mesh, PartitionSpec as P

HEAD = 128
epsilon = 1e-05
theta_base = 10000.0


def shifted(value, axis, steps):
    count = lax.axis_size(axis)
    return lax.ppermute(value, axis, [(source, source + steps) for source in range(count - steps)])


def gather_by_exchange(value, axis):
    count = lax.axis_size(axis)
    copies = jnp.broadcast_to(value[None], (count,) + value.shape)
    got = lax.all_to_all(copies, axis, 0, 0, tiled=True)
    return got.reshape((count * value.shape[0],) + value.shape[1:])


def scatter_sum(value, axis):
    count = lax.axis_size(axis)
    pieces = value.reshape((count, value.shape[0] // count) + value.shape[1:])
    got = lax.all_to_all(pieces, axis, 0, 0, tiled=True)
    return jnp.sum(got.astype(jnp.float32), axis=0)


def layer_norm(rows):
    values = rows.astype(jnp.float32)
    centre = jnp.mean(values, axis=-1, keepdims=True)
    spread = jnp.mean(jnp.square(values - centre), axis=-1, keepdims=True)
    return (values - centre) * lax.rsqrt(spread + epsilon)


def prompt_coords(first, count, lengths):
    where = first + jnp.arange(count)
    ends = jnp.cumsum(lengths)
    passed = (ends[None, :] <= where[:, None]).astype(jnp.int32)
    prompt = jnp.sum(passed, axis=1)
    offset = where - jnp.sum(passed * lengths[None, :], axis=1)
    prompt = jnp.where(where < 0, -1, prompt)
    return (prompt, offset, where)


def rotate(values, offset):
    half = values.shape[-1] // 2
    freqs = jnp.power(theta_base, -jnp.arange(half, dtype=jnp.float32) * 2.0 / values.shape[-1])
    angles = offset.astype(jnp.float32)[:, None] * freqs[None, :]
    cosine = jnp.cos(angles)[:, None, :]
    sine = jnp.sin(angles)[:, None, :]
    first_half = values[..., :half]
    second_half = values[..., half:]
    return jnp.concatenate(
        [first_half * cosine - second_half * sine, second_half * cosine + first_half * sine],
        axis=-1,
    )


def on_device(tokens, lengths, w_query, w_key, w_value, w_out, w_gate, w_up, w_down):
    half_type = jnp.bfloat16
    dp = ("y", "r")
    mp = "mp"
    rows = tokens.shape[0]
    narrow = w_query.shape[1]
    shard_rows = w_query.shape[0]
    heads_dev = narrow // HEAD
    dp_index = lax.axis_index(dp)
    mp_index = lax.axis_index(mp)
    mp_size = lax.axis_size(mp)
    y_size = lax.axis_size("y")
    r_size = lax.axis_size("r")
    reach = lax.axis_size(dp) // 2
    down_rows = w_down.shape[0]
    per_mp = down_rows // mp_size
    units_shard = w_gate.shape[1]
    blocks = units_shard // down_rows

    def unit_pieces(w):
        pieces = w.astype(half_type).reshape(shard_rows, blocks, mp_size, per_mp)
        return jnp.transpose(pieces, (2, 0, 1, 3))

    outgoing = [
        unit_pieces(w_gate),
        unit_pieces(w_up),
        w_down.astype(half_type).reshape(mp_size, per_mp, narrow),
        jnp.broadcast_to(w_out.astype(half_type)[None], (mp_size,) + w_out.shape),
    ]
    flat = jnp.concatenate([p.reshape(mp_size, -1) for p in outgoing], axis=1)
    got = lax.all_to_all(flat, mp, 0, 0, tiled=True)
    kv_shard = jnp.concatenate([w.astype(half_type) for w in (w_key, w_value)], axis=1)
    got, kv_shard = lax.optimization_barrier((got, kv_shard))
    pieces = []
    at = 0
    for p in outgoing:
        size = p[0].size
        pieces.append(got[:, at : at + size].reshape(p.shape))
        at += size
    gate_got, up_got, down_got, out_got = pieces

    def unit_columns(got_w):
        return jnp.transpose(got_w, (1, 0, 2, 3)).reshape(shard_rows, mp_size * blocks * per_mp)

    gate_shard = unit_columns(gate_got)
    up_shard = unit_columns(up_got)
    down_shard = jnp.transpose(down_got, (1, 0, 2)).reshape(per_mp, mp_size * narrow)
    units = gate_shard.shape[1]
    rest_shard = jnp.concatenate(
        [w_query.astype(half_type), gate_shard, up_shard, down_shard.reshape(shard_rows, -1)],
        axis=1,
    )
    out_full_rows = jnp.transpose(out_got, (1, 0, 2)).reshape(shard_rows, mp_size * narrow)
    swap = [(a * mp_size + b, b * mp_size + a) for a in range(y_size) for b in range(mp_size)]
    out_swapped = lax.ppermute(out_full_rows, ("y", mp), swap)
    server_out = gather_by_exchange(out_swapped, "r")
    kv_full = gather_by_exchange(kv_shard, dp)
    rest_full = lax.all_gather(rest_shard, dp, axis=0, tiled=True)
    normed = layer_norm(tokens).astype(half_type)
    joined_kv = jnp.dot(normed, kv_full, preferred_element_type=jnp.float32)
    q_prompt, q_offset, q_where = prompt_coords(dp_index * rows, rows, lengths)
    shaped = joined_kv.reshape(rows, 2, heads_dev, HEAD)
    keys = rotate(shaped[:, 0], q_offset).astype(half_type)
    values = shaped[:, 1].astype(half_type)
    own_pair = jnp.transpose(jnp.stack((keys, values)), (0, 2, 1, 3))
    plane = r_size
    back_one = shifted(own_pair, dp, plane)
    back_two = shifted(own_pair, dp, 2 * plane)
    own_first = dp_index * rows
    scale = 1.0 / HEAD**0.5

    def online_step(state, pair, first):
        accum, total, top = state
        k_prompt, k_offset, k_where = prompt_coords(first, rows, lengths)
        scores = (
            jnp.einsum("hqd,hkd->hqk", query, pair[0], preferred_element_type=jnp.float32) * scale
        )
        allowed = (q_prompt[:, None] == k_prompt[None, :]) & (k_where[None, :] <= q_where[:, None])
        scores = jnp.where(allowed[None], scores, -jnp.inf)
        new_top = jnp.maximum(top, jnp.max(scores, axis=-1, keepdims=True))
        fade = jnp.exp(top - new_top)
        weights = jnp.exp(scores - new_top)
        probs = weights.astype(half_type)
        product = jnp.einsum("hqk,hkd->hqd", probs, pair[1], preferred_element_type=jnp.float32)
        accum = accum * fade + product
        total = total * fade + jnp.sum(weights, axis=-1, keepdims=True)
        return (accum, total, new_top)

    state = (
        jnp.zeros((heads_dev, rows, HEAD), jnp.float32),
        jnp.zeros((heads_dev, rows, 1), jnp.float32),
        jnp.full((heads_dev, rows, 1), -jnp.inf, jnp.float32),
    )
    r_index = lax.axis_index("r")
    later = r_index < jnp.arange(plane)
    nearer = jnp.where(later[:, None, None, None, None], own_pair[None], back_two[None])
    payload = jnp.stack(
        (nearer, jnp.broadcast_to(back_one[None], (plane,) + back_one.shape)), axis=1
    )
    received = lax.all_to_all(payload, "r", 0, 0, tiled=True)
    q_full = rest_full[:, :narrow]
    server_gate = rest_full[:, narrow : narrow + units]
    server_up = rest_full[:, narrow + units : narrow + 2 * units]
    server_down = rest_full[:, narrow + 2 * units :].reshape(units, -1)
    received, q_full, server_gate, server_up, server_down = lax.optimization_barrier(
        (received, q_full, server_gate, server_up, server_down)
    )
    joined_q = jnp.dot(normed, q_full, preferred_element_type=jnp.float32)
    query = rotate(joined_q.reshape(rows, heads_dev, HEAD), q_offset).astype(half_type)
    query = jnp.transpose(query, (1, 0, 2))
    state = online_step(state, own_pair, own_first)

    def slot_step(back, state):
        source = lax.rem(r_index - back + 2 * plane, plane)
        middle = jnp.logical_and(back > r_index, back <= r_index + plane).astype(jnp.int32)
        pair = received[source, middle]
        return online_step(state, pair, own_first - back * rows)

    state = lax.fori_loop(1, reach + 1, slot_step, state)
    accum, total, top = state
    context = jnp.transpose((accum / total).astype(half_type), (1, 0, 2)).reshape(rows, narrow)
    partial_out = jnp.dot(context, server_out, preferred_element_type=jnp.float32)
    attended = scatter_sum(partial_out.astype(half_type), mp)
    slab = rows // mp_size
    own_tokens = lax.dynamic_slice_in_dim(tokens, mp_index * slab, slab, 0)
    mixed = (own_tokens.astype(jnp.float32) + attended).astype(half_type)
    normed_own = layer_norm(mixed).astype(half_type)
    normed_two = gather_by_exchange(normed_own, mp)
    gate = jnp.dot(normed_two, server_gate, preferred_element_type=jnp.float32)
    upper = jnp.dot(normed_two, server_up, preferred_element_type=jnp.float32)
    hidden = (jax.nn.silu(gate) * upper).astype(half_type)
    partial_down = jnp.dot(hidden, server_down, preferred_element_type=jnp.float32)
    share = scatter_sum(partial_down.astype(half_type), mp)
    return (mixed.astype(jnp.float32) + share).astype(half_type)


def solution(mesh):
    dp_size, mp_size = mesh.devices.shape
    y_size = mesh.devices.shape[0] // 8 if dp_size % 8 == 0 else 1
    fine = Mesh(mesh.devices.reshape(y_size, dp_size // y_size, mp_size), ("y", "r", "mp"))
    dp = ("y", "r")
    in_specs = (
        P(dp, None),
        P(),
        P(dp, "mp"),
        P(dp, "mp"),
        P(dp, "mp"),
        P(dp, "mp"),
        P(dp, "mp"),
        P(dp, "mp"),
        P(dp, "mp"),
    )
    out_specs = P(("y", "r", "mp"), None)
    return jax.shard_map(
        on_device, mesh=fine, in_specs=in_specs, out_specs=out_specs, check_vma=False
    )
```

profile of v0, /device:TPU:1, one launch (start us, length us, event | category | flops | bytes accessed | tf_op | source)
XLA Modules:
  0.0 446.5 jit_solution(5128202686256242654)
XLA Ops:
  12.6 1.5 reduce
  14.1 1.5 reshape.429
  15.6 4.9 %all-to-all-start = ((bf16[4,2,40960]{2,1,0:T(2,128)(2,1)}), bf16[4,2,40960]{2,1,0:T(2,128)(2,1)S(1)}, u32[]{:S(2)}, u32[]{:S(2)}) async-start(bf16[4,2,40960]{2,1,0:T(2,128)(2,1)} %reshape.429), calls=%async_computation | async-start | bytes 1310720 | tf_op jit(solution)/shard_map/all_to_all | solution.py:91
  20.7 9.2 %all-to-all-done = bf16[4,2,40960]{2,1,0:T(2,128)(2,1)S(1)} async-done(((bf16[4,2,40960]{2,1,0:T(2,128)(2,1)}), bf16[4,2,40960]{2,1,0:T(2,128)(2,1)S(1)}, u32[]{:S(2)}, u32[]{:S(2)}) %all-to-all-start) | async-done | bytes 655392 | tf_op jit(solution)/shard_map/all_to_all | solution.py:91
  34.4 2.6 broadcast_in_dim.188
  36.9 10.9 %all-to-all-start.1 = ((bf16[32,64,1024]{2,1,0:T(8,128)(2,1)}), bf16[32,64,1024]{2,1,0:T(8,128)(2,1)}, u32[]{:S(2)}, u32[]{:S(2)}) async-start(bf16[32,64,1024]{2,1,0:T(8,128)(2,1)} %broadcast_in_dim.188), calls=%async_computation.1 | async-start | bytes 8388608 | tf_op jit(solution)/shard_map/all_to_all | solution.py:19
  49.1 64.7 %all-to-all-done.1 = bf16[32,64,1024]{2,1,0:T(8,128)(2,1)} async-done(((bf16[32,64,1024]{2,1,0:T(8,128)(2,1)}), bf16[32,64,1024]{2,1,0:T(8,128)(2,1)}, u32[]{:S(2)}, u32[]{:S(2)}) %all-to-all-start.1) | async-done | bytes 4194336 | tf_op jit(solution)/shard_map/all_to_all | solution.py:19
  113.8 6.5 %copy.139 = bf16[1024,2048]{1,0:T(8,128)(2,1)} copy(bf16[1024,2048]{0,1:T(8,128)(2,1)} %bitcast.10) | data formatting | bytes 8388608 | tf_op jit(solution)/shard_map/dot_general | solution.py:120
  120.3 3.6 fusion.17
  124.1 3.0 collective-permute-start.1
  127.1 1.5 collective-permute-start
  129.6 11.8 %collective-permute-done.1 = bf16[2,4,256,128]{2,3,1,0:T(8,128)(2,1)} collective-permute-done((bf16[2,4,256,128]{2,3,1,0:T(8,128)(2,1)S(1)}, bf16[2,4,256,128]{2,3,1,0:T(8,128)(2,1)}, u32[]{:S(2)}, u32[]{:S(2)}) %collective-permute-start.1) | collective-permute-done | bytes 524320 | tf_op jit(solution)/shard_map/ppermute | solution.py:13
  141.5 2.1 copy.142
  143.5 9.2 %collective-permute-done = bf16[2,4,256,128]{2,3,1,0:T(8,128)(2,1)S(1)} collective-permute-done((bf16[2,4,256,128]{2,3,1,0:T(8,128)(2,1)S(1)}, bf16[2,4,256,128]{2,3,1,0:T(8,128)(2,1)S(1)}, u32[]{:S(2)}, u32[]{:S(2)}) %collective-permute-start) | collective-permute-done | bytes 524320 | tf_op jit(solution)/shard_map/ppermute | solution.py:13
  153.7 1.8 broadcast_select_fusion
  155.5 3.0 stack_broadcast_in_dim.2
  158.5 6.8 %pad_maximum_fusion = bf16[8,2,2,4,256,128]{5,4,3,2,1,0:T(8,128)(2,1)} fusion(bf16[8,1,2,4,256,128]{5,4,3,2,1,0:T(8,128)(2,1)} %stack_broadcast_in_dim.2, bf16[8,1,2,4,256,128]{5,4,3,2,1,0:T(8,128)(2,1)S(1)} %broadcast_select_fusion), kind=kLoop, calls=%fused_computation.22 | loop fusion | flops 4194304 | bytes 16777216 | tf_op jit(solution)/shard_map/stack | solution.py:157
  165.3 5.0 %all-to-all-start.2 = ((bf16[8,2,2,4,256,128]{5,4,3,2,1,0:T(8,128)(2,1)}), bf16[8,2,2,4,256,128]{5,4,3,2,1,0:T(8,128)(2,1)}, u32[]{:S(2)}, u32[]{:S(2)}) async-start(bf16[8,2,2,4,256,128]{5,4,3,2,1,0:T(8,128)(2,1)} %pad_maximum_fusion), calls=%async_computation.2 | async-start | bytes 16777216 | tf_op jit(solution)/shard_map/all_to_all | solution.py:160
  170.6 4.8 %collective-permute-start.2 = (bf16[64,2048]{1,0:T(8,128)(2,1)S(1)}, bf16[64,2048]{1,0:T(8,128)(2,1)S(1)}, u32[]{:S(2)}, u32[]{:S(2)}) collective-permute-start(bf16[64,2048]{1,0:T(8,128)(2,1)S(1)} %bitcast.142), channel_id=1, source_target_pairs={{0,0},{1,32},{2,64},{3,96},{32,1},{33,33},{34,65},{35,97},{64,2},{... | collective-permute-start | bytes 786440 | tf_op jit(solution)/shard_map/ppermute | solution.py:115
  175.4 122.5 %all-gather.2.cloned.1.call-done = bf16[2048,3584]{1,0:T(8,128)(2,1)} async-done(((bf16[64,3584]{1,0:T(8,128)(2,1)}), bf16[2048,3584]{1,0:T(8,128)(2,1)}) %all-gather.2.cloned.1.call-update) | async-done | bytes 14680080 | tf_op jit(solution)/shard_map/all_gather | solution.py:118
  297.9 9.1 %fusion.39 = (bf16[2048,1024]{1,0:T(8,128)(2,1)}, bf16[2048,1024]{1,0:T(8,128)(2,1)}, bf16[2048,1024]{1,0:T(8,128)(2,1)}) fusion(bf16[2048,3584]{1,0:T(8,128)(2,1)} %all-gather.2.cloned.1.call-done), kind=kLoop, calls=%fused_computation.95 | loop fusion | bytes 25165824 | tf_op jit(solution)/shard_map/slice | solution.py:164
  307.0 7.1 %reshape.418 = bf16[1024,2048]{1,0:T(8,128)(2,1)} reshape(bf16[2048,1024]{1,0:T(8,128)(2,1)} %get-tuple-element.444) | data formatting | bytes 8388608 | tf_op jit(solution)/shard_map/reshape | solution.py:164
  314.1 1.7 broadcast_in_dim.195
  315.7 4.5 %all-to-all-start.3 = ((bf16[8,64,2048]{2,1,0:T(8,128)(2,1)}), bf16[8,64,2048]{2,1,0:T(8,128)(2,1)}, u32[]{:S(2)}, u32[]{:S(2)}) async-start(bf16[8,64,2048]{2,1,0:T(8,128)(2,1)} %broadcast_in_dim.195), calls=%async_computation.3 | async-start | bytes 4194304 | tf_op jit(solution)/shard_map/all_to_all | solution.py:19
  323.1 1.3 convolution_add_fusion.1
  324.4 51.2 %while.21 = (s32[]{:T(128)}, f32[4,256,128]{2,1,0:T(8,128)S(1)}, f32[4,256,1]{1,0,2:T(4,128)S(1)}, f32[4,256,1]{1,0,2:T(4,128)S(1)}, s32[256]{0:T(256)S(1)}, /*i...) while((s32[]{:T(128)}, f32[4,256,128]{2,1,0:T(8,128)S(1)}, ...), condition=%wide.region_11.12_spmd.clone.clone, body=%wide.region_7.11_spmd.clone.clone.sunk | while | flops 136518688 | bytes 5188022 | solution.py:179
  326.2 1.4 convolution_add_fusion.3
  329.4 1.4 convolution_add_fusion.3
  332.6 1.4 convolution_add_fusion.3
  335.8 1.4 convolution_add_fusion.3
  339.0 1.4 convolution_add_fusion.3
  342.2 1.4 convolution_add_fusion.3
  345.4 1.4 convolution_add_fusion.3
  348.6 1.4 convolution_add_fusion.3
  351.8 1.4 convolution_add_fusion.3
  355.0 1.4 convolution_add_fusion.3
  358.2 1.4 convolution_add_fusion.3
  361.4 1.4 convolution_add_fusion.3
  364.6 1.4 convolution_add_fusion.3
  367.8 1.4 convolution_add_fusion.3
  371.0 1.4 convolution_add_fusion.3
  374.2 1.4 convolution_add_fusion.3
  376.0 3.4 convolution_convert_fusion
  379.4 3.9 all-to-all-start.4
  383.3 13.6 %all-to-all-done.4 = bf16[4,64,2048]{2,1,0:T(8,128)(2,1)S(1)} async-done(((bf16[4,64,2048]{2,1,0:T(8,128)(2,1)}), bf16[4,64,2048]{2,1,0:T(8,128)(2,1)S(1)}, u32[]{:S(2)}, u32[]{:S(2)}) %all-to-all-start.4) | async-done | bytes 1048608 | tf_op jit(solution)/shard_map/all_to_all | solution.py:26
  397.8 16.8 %all_to_all.42 = bf16[4,64,2048]{2,1,0:T(8,128)(2,1)S(1)} all-to-all(bf16[4,64,2048]{2,1,0:T(8,128)(2,1)S(1)} %broadcast_in_dim.196), channel_id=1, replica_groups=mesh['y'=4,'r'=8,'mp'=4] {'mp'}, dimensions={0} | all-to-all | bytes 2097152 | tf_op jit(solution)/shard_map/all_to_all | solution.py:19
  415.9 5.9 %convolution_convert_fusion.1 = bf16[256,2048]{1,0:T(8,128)(2,1)S(1)} fusion(bf16[1024,2048]{1,0:T(8,128)(2,1)} %reshape.418, bf16[256,2048]{1,0:T(8,128)(2,1)S(1)} %bitcast.134, bf16[2048,1024]{1,0:T(8,128)(2,1)} %get-tuple-element.280, f32[256,1024]{1,0:T(8,128)S(1)} %fusion.42), kind=kOutput, calls=%fused_computation.27 | convolution fusion | flops 2149580800 | bytes 11534336 | tf_op jit(solution)/shard_map/dot_general | solution.py:192
  421.8 16.9 %all_to_all.43 = bf16[4,64,2048]{2,1,0:T(8,128)(2,1)S(1)} all-to-all(bf16[4,64,2048]{2,1,0:T(8,128)(2,1)S(1)} %bitcast.135), channel_id=1, replica_groups=mesh['y'=4,'r'=8,'mp'=4] {'mp'}, dimensions={0} | all-to-all | bytes 2097152 | tf_op jit(solution)/shard_map/all_to_all | solution.py:26
  (238 shorter events, 47.6 us)
Async XLA Ops:
  6.5 4.1 copy-start.4
  12.1 8.4 %copy-start.5 = (f32[64,512]{1,0:T(8,128)S(1)}, f32[64,512]{1,0:T(8,128)}, u32[]{:S(2)}) copy-start(f32[64,512]{1,0:T(8,128)} %param.13) | copy-start | bytes 393220
  12.6 8.1 %copy-start.6 = (f32[64,512]{1,0:T(8,128)S(1)}, f32[64,512]{1,0:T(8,128)}, u32[]{:S(2)}) copy-start(f32[64,512]{1,0:T(8,128)} %param.14) | copy-start | bytes 393220
  12.6 8.1 %copy-start.7 = (f32[64,512]{1,0:T(8,128)S(1)}, f32[64,512]{1,0:T(8,128)}, u32[]{:S(2)}) copy-start(f32[64,512]{1,0:T(8,128)} %param.15) | copy-start | bytes 393220
  15.6 14.3 %all-to-all-start = ((bf16[4,2,40960]{2,1,0:T(2,128)(2,1)}), bf16[4,2,40960]{2,1,0:T(2,128)(2,1)S(1)}, u32[]{:S(2)}, u32[]{:S(2)}) async-start(bf16[4,2,40960]{2,1,0:T(2,128)(2,1)} %reshape.429), calls=%async_computation | async-start | bytes 1310720 | tf_op jit(solution)/shard_map/all_to_all | solution.py:91
  20.5 277.4 %all-gather.2.cloned.1.call-start = ((), (), s32[]{:S(2)}) async-start(), calls=%async_computation.7 | async-start | bytes 15138816 | tf_op jit(solution)/shard_map/all_gather | solution.py:118
  36.9 10.9 %copy-start.8 = (s32[4]{0:T(128)S(1)}, s32[4]{0:T(128)}, u32[]{:S(2)}) copy-start(s32[4]{0:T(128)} %param.12) | copy-start | bytes 52
  36.9 11.2 %copy-start = (bf16[256,2048]{1,0:T(8,128)(2,1)S(1)}, bf16[256,2048]{1,0:T(8,128)(2,1)}, u32[]{:S(2)}) copy-start(bf16[256,2048]{1,0:T(8,128)(2,1)} %param.11) | copy-start | bytes 3145732
  36.9 76.8 %all-to-all-start.1 = ((bf16[32,64,1024]{2,1,0:T(8,128)(2,1)}), bf16[32,64,1024]{2,1,0:T(8,128)(2,1)}, u32[]{:S(2)}, u32[]{:S(2)}) async-start(bf16[32,64,1024]{2,1,0:T(8,128)(2,1)} %broadcast_in_dim.188), calls=%async_computation.1 | async-start | bytes 8388608 | tf_op jit(solution)/shard_map/all_to_all | solution.py:19
  124.1 28.6 %copy-start.2 = (bf16[2,4,256,128]{2,3,1,0:T(8,128)(2,1)}, bf16[2,4,256,128]{2,3,1,0:T(8,128)(2,1)S(1)}, u32[]{:S(2)}) copy-start(bf16[2,4,256,128]{2,3,1,0:T(8,128)(2,1)S(1)} %maximum_bitcast_fusion.1) | copy-start | bytes 1572868
  124.1 17.4 %collective-permute-start.1 = (bf16[2,4,256,128]{2,3,1,0:T(8,128)(2,1)S(1)}, bf16[2,4,256,128]{2,3,1,0:T(8,128)(2,1)}, u32[]{:S(2)}, u32[]{:S(2)}) collective-permute-start(bf16[2,4,256,128]{2,3,1,0:T(8,128)(2,1)S(1)} %maximum_bitcast_fusion.1), channel_id=1, source_target_pairs={{0,32},{4,36},{8,40},{12,44},{16,48},{20,52},{24,56},{28,60},{32,6... | collective-permute-start | bytes 1572872 | tf_op jit(solution)/shard_map/ppermute | solution.py:13
  127.1 25.6 %collective-permute-start = (bf16[2,4,256,128]{2,3,1,0:T(8,128)(2,1)S(1)}, bf16[2,4,256,128]{2,3,1,0:T(8,128)(2,1)S(1)}, u32[]{:S(2)}, u32[]{:S(2)}) collective-permute-start(bf16[2,4,256,128]{2,3,1,0:T(8,128)(2,1)S(1)} %maximum_bitcast_fusion.1), channel_id=1, source_target_pairs={{0,64},{4,68},{8,72},{12,76},{16,80},{20,84},{24,88},{28,92},{32,9... | collective-permute-start | bytes 1572872 | tf_op jit(solution)/shard_map/ppermute | solution.py:13
  153.7 1.8 copy-start.3
  165.3 148.8 %all-to-all-start.2 = ((bf16[8,2,2,4,256,128]{5,4,3,2,1,0:T(8,128)(2,1)}), bf16[8,2,2,4,256,128]{5,4,3,2,1,0:T(8,128)(2,1)}, u32[]{:S(2)}, u32[]{:S(2)}) async-start(bf16[8,2,2,4,256,128]{5,4,3,2,1,0:T(8,128)(2,1)} %pad_maximum_fusion), calls=%async_computation.2 | async-start | bytes 16777216 | tf_op jit(solution)/shard_map/all_to_all | solution.py:160
  170.6 143.5 %collective-permute-start.2 = (bf16[64,2048]{1,0:T(8,128)(2,1)S(1)}, bf16[64,2048]{1,0:T(8,128)(2,1)S(1)}, u32[]{:S(2)}, u32[]{:S(2)}) collective-permute-start(bf16[64,2048]{1,0:T(8,128)(2,1)S(1)} %bitcast.142), channel_id=1, source_target_pairs={{0,0},{1,32},{2,64},{3,96},{32,1},{33,33},{34,65},{35,97},{64,2},{... | collective-permute-start | bytes 786440 | tf_op jit(solution)/shard_map/ppermute | solution.py:115
  315.7 4.5 %slice-start = ((bf16[2048,3584]{1,0:T(8,128)(2,1)}), bf16[2048,512]{1,0:T(8,128)(2,1)S(1)}, s32[]{:S(2)}) async-start(bf16[2048,3584]{1,0:T(8,128)(2,1)} %all-gather.2.cloned.1.call-done), calls=%async_computation.8 | async-start | bytes 4194304 | tf_op jit(solution)/shard_map/slice | solution.py:161
  315.7 60.2 %all-to-all-start.3 = ((bf16[8,64,2048]{2,1,0:T(8,128)(2,1)}), bf16[8,64,2048]{2,1,0:T(8,128)(2,1)}, u32[]{:S(2)}, u32[]{:S(2)}) async-start(bf16[8,64,2048]{2,1,0:T(8,128)(2,1)} %broadcast_in_dim.195), calls=%async_computation.3 | async-start | bytes 4194304 | tf_op jit(solution)/shard_map/all_to_all | solution.py:19
  379.4 17.5 %all-to-all-start.4 = ((bf16[4,64,2048]{2,1,0:T(8,128)(2,1)}), bf16[4,64,2048]{2,1,0:T(8,128)(2,1)S(1)}, u32[]{:S(2)}, u32[]{:S(2)}) async-start(bf16[4,64,2048]{2,1,0:T(8,128)(2,1)} %bitcast.35), calls=%async_computation.4 | async-start | bytes 2097152 | tf_op jit(solution)/shard_map/all_to_all | solution.py:26
  397.2 17.4 %copy-start.1 = (bf16[2048,1024]{1,0:T(8,128)(2,1)S(1)}, bf16[2048,1024]{1,0:T(8,128)(2,1)}, u32[]{:S(2)}) copy-start(bf16[2048,1024]{1,0:T(8,128)(2,1)} %get-tuple-element.279) | copy-start | bytes 12582916
Sparse Core Ops, SparseCore 0:
  34.5 263.3 all-gather.1
where the time goes:
time: 449 us; the launch traced here: 446 us
  waiting for transfers between devices  231 us (51%)
  matrix products  60.9 us (14%)
  local copies, waits for them, and re-layouts  44.3 us (10%)
  starting transfers between devices  38.4 us (9%)
  blocking collectives  33.7 us (8%)
  other arithmetic  22.8 us (5%)
  between operations  13.9 us (3%)
    all_gather x1, waiting for transfers between devices, on_device(): rest_full = lax.all_gather(rest_shard, dp, axis=0, tiled=True)  123 us
    all_to_all x2, waiting for transfers between devices, gather_by_exchange(): got = lax.all_to_all(copies, axis, 0, 0, tiled=True)  64.7 us
    dot_general x17, matrix products, online_step(): jnp.einsum('hqk,hkd->hqd', probs, pair[1], preferred_element_type=jnp.flo...  24 us
    dot_general x17, matrix products, online_step(): jnp.einsum('hqd,hkd->hqk', query, pair[0], preferred_element_type=jnp.flo...  21.7 us
    ppermute x2, waiting for transfers between devices, shifted(): lax.ppermute(value, axis, [(source, source + steps) for source in range(c...  21 us
    all_to_all x1, blocking collectives, scatter_sum(): got = lax.all_to_all(pieces, axis, 0, 0, tiled=True)  16.9 us
    all_to_all x1, blocking collectives, gather_by_exchange(): got = lax.all_to_all(copies, axis, 0, 0, tiled=True)  16.8 us
    all_to_all x2, starting transfers between devices, gather_by_exchange(): got = lax.all_to_all(copies, axis, 0, 0, tiled=True)  15.3 us
  transfers between devices with their start and end apart: 9, of which 6 were waited for; matrix products, arithmetic and copies ran while one was open for 23% of the time, Pallas kernels for 0%

commit v1 on v0

--- a/solution.py
+++ b/solution.py
@@ -115,7 +115,9 @@
     out_swapped = lax.ppermute(out_full_rows, ("y", mp), swap)
     server_out = gather_by_exchange(out_swapped, "r")
     kv_full = gather_by_exchange(kv_shard, dp)
-    rest_full = lax.all_gather(rest_shard, dp, axis=0, tiled=True)
+    rest_full = jnp.concatenate(
+        lax.all_to_all(jnp.stack([rest_shard] * lax.axis_size(dp)), dp, 0, 0), axis=0
+    )
     normed = layer_norm(tokens).astype(half_type)
     joined_kv = jnp.dot(normed, kv_full, preferred_element_type=jnp.float32)
     q_prompt, q_offset, q_where = prompt_coords(dp_index * rows, rows, lengths)

time: 449 us -> 607 us (1.35)
  waiting for transfers between devices: 231 us -> 368 us
  starting transfers between devices: 38.4 us -> 60.5 us
  between operations: 13.9 us -> 0.54 us
  local copies, waits for them, and re-layouts: 44.3 us -> 54.4 us
    ppermute x2, waiting for transfers between devices: 21 us -> 219 us  [shifted(): lax.ppermute(value, axis, [(source, source + steps) for source in range(c...]
    all_gather x1 -> x0, waiting for transfers between devices: 123 us -> none  [on_device(): rest_full = lax.all_gather(rest_shard, dp, axis=0, tiled=True)]
    all_to_all x1, waiting for transfers between devices: 0.01 us -> 71 us  [on_device(): received = lax.all_to_all(payload, 'r', 0, 0, tiled=True)]
    all_to_all x1, starting transfers between devices: 3.94 us -> 19.4 us  [scatter_sum(): got = lax.all_to_all(pieces, axis, 0, 0, tiled=True)]
    all_to_all x2, waiting for transfers between devices: 64.7 us -> 55.4 us  [gather_by_exchange(): got = lax.all_to_all(copies, axis, 0, 0, tiled=True)]
    another operation x0 -> x1, local copies, waits for them, and re-layouts: none -> 6.85 us  [on_device(): jnp.stack([rest_shard] * lax.axis_size(dp))]
  transfers between devices with their start and end apart: 9 -> 9, of which waited for: 6 -> 6; matrix products, arithmetic and copies ran while one was open for 23% -> 17% of each run, Pallas kernels for 0% -> 0%
where the time goes in v1:
time: 607 us; the launch traced here: 602 us
  waiting for transfers between devices  368 us (61%)
  starting transfers between devices  60.5 us (10%)
  matrix products  60.4 us (10%)
  local copies, waits for them, and re-layouts  54.4 us (9%)
  blocking collectives  34 us (6%)
  other arithmetic  22 us (4%)
    ppermute x2, waiting for transfers between devices, shifted(): lax.ppermute(value, axis, [(source, source + steps) for source in range(c...  219 us
    all_to_all x1, waiting for transfers between devices, on_device(): received = lax.all_to_all(payload, 'r', 0, 0, tiled=True)  71 us
    all_to_all x2, waiting for transfers between devices, gather_by_exchange(): got = lax.all_to_all(copies, axis, 0, 0, tiled=True)  55.4 us
    dot_general x17, matrix products, online_step(): jnp.einsum('hqk,hkd->hqd', probs, pair[1], preferred_element_type=jnp.flo...  23 us
    dot_general x17, matrix products, online_step(): jnp.einsum('hqd,hkd->hqk', query, pair[0], preferred_element_type=jnp.flo...  20.7 us
    all_to_all x1, starting transfers between devices, scatter_sum(): got = lax.all_to_all(pieces, axis, 0, 0, tiled=True)  19.4 us
    all_to_all x1, blocking collectives, gather_by_exchange(): got = lax.all_to_all(copies, axis, 0, 0, tiled=True)  17.1 us
    all_to_all x1, blocking collectives, scatter_sum(): got = lax.all_to_all(pieces, axis, 0, 0, tiled=True)  16.9 us
  transfers between devices with their start and end apart: 9, of which 6 were waited for; matrix products, arithmetic and copies ran while one was open for 17% of the time, Pallas kernels for 0%

profile of v1, /device:TPU:1, one launch (start us, length us, event | category | flops | bytes accessed | tf_op | source)
XLA Modules:
  0.0 601.6 jit_solution(16259104194180619939)
XLA Ops:
  5.2 1.5 reduce
  6.7 1.5 reshape.435
  8.2 4.9 all-to-all-start
  13.3 9.2 %all-to-all-done = bf16[4,2,40960]{2,1,0:T(2,128)(2,1)S(1)} async-done(((bf16[4,2,40960]{2,1,0:T(2,128)(2,1)}), bf16[4,2,40960]{2,1,0:T(2,128)(2,1)S(1)}, u32[]{:S(2)}, u32[]{:S(2)}) %all-to-all-start) | async-done | bytes 655392 | tf_op jit(solution)/shard_map/all_to_all | solution.py:91
  24.0 2.5 broadcast_in_dim.188
  26.4 10.7 %all-to-all-start.1 = ((bf16[32,64,1024]{2,1,0:T(8,128)(2,1)}), bf16[32,64,1024]{2,1,0:T(8,128)(2,1)}, u32[]{:S(2)}, u32[]{:S(2)}) async-start(bf16[32,64,1024]{2,1,0:T(8,128)(2,1)} %broadcast_in_dim.188), calls=%async_computation.1 | async-start | bytes 8388608 | tf_op jit(solution)/shard_map/all_to_all | solution.py:19
  39.4 55.4 %all-to-all-done.1 = bf16[32,64,1024]{2,1,0:T(8,128)(2,1)} async-done(((bf16[32,64,1024]{2,1,0:T(8,128)(2,1)}), bf16[32,64,1024]{2,1,0:T(8,128)(2,1)}, u32[]{:S(2)}, u32[]{:S(2)}) %all-to-all-start.1) | async-done | bytes 4194336 | tf_op jit(solution)/shard_map/all_to_all | solution.py:19
  94.7 6.8 %stack.8 = bf16[32,64,3584]{2,1,0:T(8,128)(2,1)} broadcast(bf16[64,3584]{1,0:T(8,128)(2,1)S(1)} %copy.128), dimensions={1,2} | broadcast | bytes 15138816 | tf_op jit(solution)/shard_map/stack | solution.py:119
  101.6 6.0 all-to-all-start.3
  108.8 6.5 %copy.119 = bf16[1024,2048]{1,0:T(8,128)(2,1)} copy(bf16[1024,2048]{0,1:T(8,128)(2,1)} %bitcast.10) | data formatting | bytes 8388608 | tf_op jit(solution)/shard_map/dot_general | solution.py:122
  115.4 3.6 fusion.17
  119.1 3.8 collective-permute-start.1
  122.9 3.5 collective-permute-start
  127.5 209.5 %collective-permute-done.1 = bf16[2,4,256,128]{2,3,1,0:T(8,128)(2,1)} collective-permute-done((bf16[2,4,256,128]{2,3,1,0:T(8,128)(2,1)S(1)}, bf16[2,4,256,128]{2,3,1,0:T(8,128)(2,1)}, u32[]{:S(2)}, u32[]{:S(2)}) %collective-permute-start.1) | collective-permute-done | bytes 524320 | tf_op jit(solution)/shard_map/ppermute | solution.py:13
  338.2 9.9 %collective-permute-done = bf16[2,4,256,128]{2,3,1,0:T(8,128)(2,1)S(1)} collective-permute-done((bf16[2,4,256,128]{2,3,1,0:T(8,128)(2,1)S(1)}, bf16[2,4,256,128]{2,3,1,0:T(8,128)(2,1)S(1)}, u32[]{:S(2)}, u32[]{:S(2)}) %collective-permute-start) | collective-permute-done | bytes 524320 | tf_op jit(solution)/shard_map/ppermute | solution.py:13
  349.2 1.7 broadcast_select_fusion
  350.9 3.0 stack_broadcast_in_dim.2
  353.9 6.3 %pad_maximum_fusion = bf16[8,2,2,4,256,128]{5,4,3,2,1,0:T(8,128)(2,1)} fusion(bf16[8,1,2,4,256,128]{5,4,3,2,1,0:T(8,128)(2,1)} %stack_broadcast_in_dim.2, bf16[8,1,2,4,256,128]{5,4,3,2,1,0:T(8,128)(2,1)S(1)} %broadcast_select_fusion), kind=kLoop, calls=%fused_computation.22 | loop fusion | flops 4194304 | bytes 16777216 | tf_op jit(solution)/shard_map/stack | solution.py:159
  360.2 5.0 all-to-all-start.2
  366.4 1.9 collective-permute-start.2
  368.3 9.1 %fusion.39 = (bf16[2048,1024]{1,0:T(8,128)(2,1)}, bf16[2048,1024]{1,0:T(8,128)(2,1)}, bf16[2048,1024]{1,0:T(8,128)(2,1)}) fusion(bf16[2048,3584]{1,0:T(8,128)(2,1)} %bitcast.23), kind=kLoop, calls=%fused_computation.95 | loop fusion | bytes 25165824 | tf_op jit(solution)/shard_map/slice | solution.py:166
  377.4 3.0 slice.93
  380.4 7.1 %reshape.424 = bf16[1024,2048]{1,0:T(8,128)(2,1)} reshape(bf16[2048,1024]{1,0:T(8,128)(2,1)} %get-tuple-element.433) | data formatting | bytes 8388608 | tf_op jit(solution)/shard_map/reshape | solution.py:166
  387.6 71.0 %all-to-all-done.2 = bf16[8,2,2,4,256,128]{5,4,3,2,1,0:T(8,128)(2,1)} async-done(((bf16[8,2,2,4,256,128]{5,4,3,2,1,0:T(8,128)(2,1)}), bf16[8,2,2,4,256,128]{5,4,3,2,1,0:T(8,128)(2,1)}, u32[]{:S(2)}, u32[]{:S(2)}) %all-to-all-start.2) | async-done | bytes 8388640 | tf_op jit(solution)/shard_map/all_to_all | solution.py:162
  458.5 1.6 broadcast_in_dim.195
  460.1 5.4 all-to-all-start.4
  465.5 2.6 fusion.35
  471.0 51.2 %while.21 = (s32[]{:T(128)}, f32[4,256,128]{2,1,0:T(8,128)S(1)}, f32[4,256,1]{1,0,2:T(4,128)S(1)}, f32[4,256,1]{1,0,2:T(4,128)S(1)}, s32[256]{0:T(256)S(1)}, /*i...) while((s32[]{:T(128)}, f32[4,256,128]{2,1,0:T(8,128)S(1)}, ...), condition=%wide.region_11.12_spmd.clone.clone, body=%wide.region_7.11_spmd.clone.clone.sunk | while | flops 136518688 | bytes 5188022 | solution.py:181
  472.6 1.4 convolution_add_fusion.3
  475.8 1.4 convolution_add_fusion.3
  479.0 1.4 convolution_add_fusion.3
  482.2 1.4 convolution_add_fusion.3
  488.6 1.4 convolution_add_fusion.3
  491.8 1.4 convolution_add_fusion.3
  498.2 1.4 convolution_add_fusion.3
  501.4 1.4 convolution_add_fusion.3
  504.6 1.4 convolution_add_fusion.3
  507.8 1.4 convolution_add_fusion.3
  511.1 1.4 convolution_add_fusion.3
  514.3 1.4 convolution_add_fusion.3
  517.5 1.4 convolution_add_fusion.3
  520.7 1.4 convolution_add_fusion.3
  522.6 3.3 convolution_convert_fusion
  525.9 19.4 %all-to-all-start.5 = ((bf16[4,64,2048]{2,1,0:T(8,128)(2,1)}), bf16[4,64,2048]{2,1,0:T(8,128)(2,1)S(1)}, u32[]{:S(2)}, u32[]{:S(2)}) async-start(bf16[4,64,2048]{2,1,0:T(8,128)(2,1)} %bitcast.124), calls=%async_computation.5 | async-start | bytes 2097152 | tf_op jit(solution)/shard_map/all_to_all | solution.py:26
  545.2 13.4 %all-to-all-done.5 = bf16[4,64,2048]{2,1,0:T(8,128)(2,1)S(1)} async-done(((bf16[4,64,2048]{2,1,0:T(8,128)(2,1)}), bf16[4,64,2048]{2,1,0:T(8,128)(2,1)S(1)}, u32[]{:S(2)}, u32[]{:S(2)}) %all-to-all-start.5) | async-done | bytes 1048608 | tf_op jit(solution)/shard_map/all_to_all | solution.py:26
  559.5 17.1 %all_to_all.47 = bf16[4,64,2048]{2,1,0:T(8,128)(2,1)S(1)} all-to-all(bf16[4,64,2048]{2,1,0:T(8,128)(2,1)S(1)} %broadcast_in_dim.196), channel_id=1, replica_groups=mesh['y'=4,'r'=8,'mp'=4] {'mp'}, dimensions={0} | all-to-all | bytes 2097152 | tf_op jit(solution)/shard_map/all_to_all | solution.py:19
  577.8 5.9 convolution_convert_fusion.1
  583.8 16.9 %all_to_all.48 = bf16[4,64,2048]{2,1,0:T(8,128)(2,1)S(1)} all-to-all(bf16[4,64,2048]{2,1,0:T(8,128)(2,1)S(1)} %bitcast.137), channel_id=1, replica_groups=mesh['y'=4,'r'=8,'mp'=4] {'mp'}, dimensions={0} | all-to-all | bytes 2097152 | tf_op jit(solution)/shard_map/all_to_all | solution.py:26
  (237 shorter events, 51.0 us)
Async XLA Ops:
  0.0 3.1 copy-start.3
  1.0 3.2 copy-start.4
  4.6 8.4 %copy-start.5 = (f32[64,512]{1,0:T(8,128)S(1)}, f32[64,512]{1,0:T(8,128)}, u32[]{:S(2)}) copy-start(f32[64,512]{1,0:T(8,128)} %param.15) | copy-start | bytes 393220
  4.7 8.5 %copy-start.6 = (f32[64,512]{1,0:T(8,128)S(1)}, f32[64,512]{1,0:T(8,128)}, u32[]{:S(2)}) copy-start(f32[64,512]{1,0:T(8,128)} %param.14) | copy-start | bytes 393220
  5.2 8.0 %copy-start.7 = (f32[64,512]{1,0:T(8,128)S(1)}, f32[64,512]{1,0:T(8,128)}, u32[]{:S(2)}) copy-start(f32[64,512]{1,0:T(8,128)} %param.13) | copy-start | bytes 393220
  8.2 14.3 %all-to-all-start = ((bf16[4,2,40960]{2,1,0:T(2,128)(2,1)}), bf16[4,2,40960]{2,1,0:T(2,128)(2,1)S(1)}, u32[]{:S(2)}, u32[]{:S(2)}) async-start(bf16[4,2,40960]{2,1,0:T(2,128)(2,1)} %reshape.435), calls=%async_computation | async-start | bytes 1310720 | tf_op jit(solution)/shard_map/all_to_all | solution.py:91
  24.0 13.2 %copy-start.2 = (bf16[4,1,81920]{2,0,1:T(4,128)(2,1)}, bf16[4,1,81920]{2,0,1:T(4,128)(2,1)S(1)}, u32[]{:S(2)}) copy-start(bf16[4,1,81920]{2,0,1:T(4,128)(2,1)S(1)} %copy.148) | copy-start | bytes 1966084
  26.4 68.3 %all-to-all-start.1 = ((bf16[32,64,1024]{2,1,0:T(8,128)(2,1)}), bf16[32,64,1024]{2,1,0:T(8,128)(2,1)}, u32[]{:S(2)}, u32[]{:S(2)}) async-start(bf16[32,64,1024]{2,1,0:T(8,128)(2,1)} %broadcast_in_dim.188), calls=%async_computation.1 | async-start | bytes 8388608 | tf_op jit(solution)/shard_map/all_to_all | solution.py:19
  101.6 6.0 copy-start.8
  101.6 6.3 %copy-start = (bf16[256,2048]{1,0:T(8,128)(2,1)S(1)}, bf16[256,2048]{1,0:T(8,128)(2,1)}, u32[]{:S(2)}) copy-start(bf16[256,2048]{1,0:T(8,128)(2,1)} %param.11) | copy-start | bytes 3145732
  101.6 258.6 %all-to-all-start.3 = ((bf16[32,64,3584]{2,1,0:T(8,128)(2,1)}), bf16[32,64,3584]{2,1,0:T(8,128)(2,1)}, u32[]{:S(2)}, u32[]{:S(2)}) async-start(bf16[32,64,3584]{2,1,0:T(8,128)(2,1)} %stack.8), calls=%async_computation.3 | async-start | bytes 29360128 | tf_op jit(solution)/shard_map/all_to_all | solution.py:119
  119.1 217.8 %collective-permute-start.1 = (bf16[2,4,256,128]{2,3,1,0:T(8,128)(2,1)S(1)}, bf16[2,4,256,128]{2,3,1,0:T(8,128)(2,1)}, u32[]{:S(2)}, u32[]{:S(2)}) collective-permute-start(bf16[2,4,256,128]{2,3,1,0:T(8,128)(2,1)S(1)} %maximum_bitcast_fusion.1), channel_id=1, source_target_pairs={{0,32},{4,36},{8,40},{12,44},{16,48},{20,52},{24,56},{28,60},{32,6... | collective-permute-start | bytes 1572872 | tf_op jit(solution)/shard_map/ppermute | solution.py:13
  122.9 225.3 %collective-permute-start = (bf16[2,4,256,128]{2,3,1,0:T(8,128)(2,1)S(1)}, bf16[2,4,256,128]{2,3,1,0:T(8,128)(2,1)S(1)}, u32[]{:S(2)}, u32[]{:S(2)}) collective-permute-start(bf16[2,4,256,128]{2,3,1,0:T(8,128)(2,1)S(1)} %maximum_bitcast_fusion.1), channel_id=1, source_target_pairs={{0,64},{4,68},{8,72},{12,76},{16,80},{20,84},{24,88},{28,92},{32,9... | collective-permute-start | bytes 1572872 | tf_op jit(solution)/shard_map/ppermute | solution.py:13
  360.2 98.3 %all-to-all-start.2 = ((bf16[8,2,2,4,256,128]{5,4,3,2,1,0:T(8,128)(2,1)}), bf16[8,2,2,4,256,128]{5,4,3,2,1,0:T(8,128)(2,1)}, u32[]{:S(2)}, u32[]{:S(2)}) async-start(bf16[8,2,2,4,256,128]{5,4,3,2,1,0:T(8,128)(2,1)} %pad_maximum_fusion), calls=%async_computation.2 | async-start | bytes 16777216 | tf_op jit(solution)/shard_map/all_to_all | solution.py:162
  366.4 21.1 %collective-permute-start.2 = (bf16[64,2048]{1,0:T(8,128)(2,1)S(1)}, bf16[64,2048]{1,0:T(8,128)(2,1)S(1)}, u32[]{:S(2)}, u32[]{:S(2)}) collective-permute-start(bf16[64,2048]{1,0:T(8,128)(2,1)S(1)} %bitcast.144), channel_id=1, source_target_pairs={{0,0},{1,32},{2,64},{3,96},{32,1},{33,33},{34,65},{35,97},{64,2},{... | collective-permute-start | bytes 786440 | tf_op jit(solution)/shard_map/ppermute | solution.py:115
  460.1 62.4 %all-to-all-start.4 = ((bf16[8,64,2048]{2,1,0:T(8,128)(2,1)}), bf16[8,64,2048]{2,1,0:T(8,128)(2,1)}, u32[]{:S(2)}, u32[]{:S(2)}) async-start(bf16[8,64,2048]{2,1,0:T(8,128)(2,1)} %broadcast_in_dim.195), calls=%async_computation.4 | async-start | bytes 4194304 | tf_op jit(solution)/shard_map/all_to_all | solution.py:19
  525.9 32.7 %all-to-all-start.5 = ((bf16[4,64,2048]{2,1,0:T(8,128)(2,1)}), bf16[4,64,2048]{2,1,0:T(8,128)(2,1)S(1)}, u32[]{:S(2)}, u32[]{:S(2)}) async-start(bf16[4,64,2048]{2,1,0:T(8,128)(2,1)} %bitcast.124), calls=%async_computation.5 | async-start | bytes 2097152 | tf_op jit(solution)/shard_map/all_to_all | solution.py:26
  558.9 17.6 %copy-start.1 = (bf16[2048,1024]{1,0:T(8,128)(2,1)S(1)}, bf16[2048,1024]{1,0:T(8,128)(2,1)}, u32[]{:S(2)}) copy-start(bf16[2048,1024]{1,0:T(8,128)(2,1)} %get-tuple-element.279) | copy-start | bytes 12582916
